TPU v7x, 32 devices: a whole 2x2x4 slice. The times are simulated.
32 devices in a mesh: groups: 2 (over y), picks: 4 (over z), heads: 4 (over x, core).
Axes of the slice: x: 2, y: 2, z: 4, core: 2. Of those that a mesh axis runs over, the one named last changes fastest.
Arguments:
- coords: float32 [3, 8192], P(None, ('groups', 'picks')), parts along dimension 1, may hold values from -1 to 1
- horizon_ids: int32 [8192], P(('groups', 'picks')), parts along dimension 0, may hold values from 0 to 63
- horizon_levels: float32 [128], P('groups'), parts along dimension 0, may hold values from -2 to 2
- latents: bfloat16 [512, 1024], replicated, may hold values from -960 to 960
- kv_weight: bfloat16 [3072, 2, 1024], P('picks', None, 'heads'), may hold values from -0.109375 to 0.109375
- cross_out: bfloat16 [1024, 1024], P('heads'), may hold values from -0.75 to 0.75
- norm_gains: float32 [2, 1024], replicated, may hold values from 0.1 to 1.9
- self_qkv: bfloat16 [3, 1024, 1024], P(None, None, 'heads'), may hold values from -0.1875 to 0.1875
- self_out: bfloat16 [1024, 1024], P(None, 'heads'), may hold values from -0.1875 to 0.1875
- dec_kv: bfloat16 [2, 1024, 1024], P(None, None, 'heads'), may hold values from -0.1875 to 0.1875
- dec_query: bfloat16 [3072, 1024], P('picks', 'heads'), may hold values from -0.109375 to 0.109375
- readout: float32 [1024], P('heads'), may hold values from -0.1875 to 0.1875
Outputs:
- field: float32 [8192], P(('groups', 'picks')), parts along dimension 0
- latents_out: float32 [1024, 1024], P('groups', 'heads'), parts along dimension 0
- grad_query: float32 [6144, 1024], P(('groups', 'picks'), 'heads'), parts along dimension 0
There are 2 independent parts, one for each index of `groups`. A program takes and returns all parts, laid end to end along the dimension named above; an argument that names none is the same for every part. Nothing has to cross between parts.
All inputs are finite; a program needn't handle non-finite values.
Results may differ from a plain program's by a relative error of at most 0.028.
Values may be sent and summed in bfloat16 or wider, within the bound.
No kernel may reach another device: no remote copies, remote signals or barrier semaphores. Data moves between devices by JAX's collectives and lax.ppermute only.
A program may use at most 64 MiB of HBM per device.

v0:
```python
import functools
import jax
import jax.numpy as jnp
from jax import lax
from jax.sharding import PartitionSpec as P

HEAD = 128
BANDS = 512
HORIZONS = 64
PI = 3.141592653589793
EPS = 1e-06
RING_MAX = 4


def encode(coords):
    freq = jnp.linspace(1.0, BANDS / 2.0, BANDS).astype(jnp.float32)
    angle = PI * freq[None, :, None] * coords[:, None, :]
    table = jnp.concatenate([jnp.sin(angle), jnp.cos(angle)], axis=0)
    return table.reshape(6 * BANDS, coords.shape[1]).T.astype(jnp.bfloat16)


def ring_gather(x, axis, n):
    if n == 1:
        return x
    if n > RING_MAX:
        return lax.all_gather(x, axis, axis=0, tiled=True)
    idx = lax.axis_index(axis)
    blocks = [x]
    for s in range(1, n):
        blocks.append(lax.ppermute(x, axis, [(i, (i - s) % n) for i in range(n)]))
    flipped = jnp.stack(blocks)
    ordered = jnp.roll(flipped, idx, axis=0)
    return ordered.reshape((n * x.shape[0],) + x.shape[1:])


def fetch_rows(kv_weight, n_picks, n_groups):
    if n_groups != 2:
        return lax.all_gather(kv_weight, "picks", axis=0, tiled=True)
    g = lax.axis_index("groups")
    rows = kv_weight.shape[0] // 2
    mine = lax.dynamic_slice_in_dim(kv_weight, g * rows, rows, 0)
    first = max(8, 2 * rows // 3 // 8 * 8)
    bounds = [(0, first), (first, rows)] if first < rows else [(0, rows)]
    own, other = ([], [])
    for lo, hi in bounds:
        gathered = lax.all_gather(mine[lo:hi], "picks", axis=0, tiled=False)
        own.append(gathered)
        other.append(lax.ppermute(gathered, "groups", [(0, 1), (1, 0)]))
    halves = jnp.stack([jnp.concatenate(own, axis=1), jnp.concatenate(other, axis=1)], axis=1)
    halves = jnp.roll(halves, g, axis=1)
    return halves.reshape((n_picks * kv_weight.shape[0],) + kv_weight.shape[1:])


def pair_sum(x, axis, n):
    if n != 4:
        return lax.psum(x, axis)
    x = x + lax.ppermute(x, axis, [(k, k ^ 1) for k in range(n)])
    return x + lax.ppermute(x, axis, [(k, k ^ 2) for k in range(n)])


def on_device(
    coords,
    horizon_ids,
    horizon_levels,
    latents,
    kv_weight,
    cross_out,
    norm_gains,
    self_qkv,
    self_out,
    dec_kv,
    dec_query,
    readout,
    *,
    n_picks,
    n_heads,
    n_groups
):
    high = lax.Precision.HIGHEST
    scale = HEAD ** (-0.5)
    count = coords.shape[1]
    width = latents.shape[1]
    lat_rows = latents.shape[0]
    local = kv_weight.shape[2]
    nheads = local // HEAD
    column = lax.axis_index("heads") * local
    enc = encode(coords)
    cross_full = ring_gather(cross_out, "heads", n_heads)
    piece = lax.all_gather(kv_weight, "picks", axis=0, tiled=True)
    cross_full, piece = lax.optimization_barrier((cross_full, piece))
    keys_vals = jnp.einsum("tf,fjc->tjc", enc, piece, preferred_element_type=jnp.float32).astype(
        jnp.bfloat16
    )
    keys = keys_vals[:, 0].reshape(count, nheads, HEAD)
    values = keys_vals[:, 1].reshape(count, nheads, HEAD)
    queries = lax.dynamic_slice_in_dim(latents, column, local, 1).reshape(lat_rows, nheads, HEAD)
    scores = jnp.einsum("lhc,thc->hlt", queries, keys, preferred_element_type=jnp.float32) * scale
    top = jnp.max(scores, axis=2)
    expo = jnp.exp(scores - top[:, :, None])
    total = jnp.sum(expo, axis=2)
    numer = jnp.einsum(
        "hlt,thc->hlc", expo.astype(jnp.bfloat16), values, preferred_element_type=jnp.float32
    )
    all_numer = lax.all_gather(numer.astype(jnp.bfloat16), "picks", axis=0, tiled=False)
    all_stats = lax.all_gather(jnp.stack([top, total]), "picks", axis=0, tiled=False)
    best = jnp.max(all_stats[:, 0], axis=0)
    factor = jnp.exp(all_stats[:, 0] - best[None])
    merged_total = jnp.sum(factor * all_stats[:, 1], axis=0)
    merged_numer = jnp.einsum(
        "phl,phlc->hlc", factor, all_numer.astype(jnp.float32), precision=high
    )
    attended = (
        (merged_numer / merged_total[:, :, None])
        .transpose(1, 0, 2)
        .reshape(lat_rows, local)
        .astype(jnp.bfloat16)
    )
    out_full = ring_gather(self_out.T, "heads", n_heads).T
    out_full, attended = lax.optimization_barrier((out_full, attended))
    dq_local, attended = lax.optimization_barrier((dec_query, attended))
    dq_full = lax.all_gather(dq_local, "picks", axis=0, tiled=True)
    attended_full = ring_gather(attended.T, "heads", n_heads).T
    whole = latents.astype(jnp.float32) + jnp.dot(
        attended_full, cross_full, preferred_element_type=jnp.float32
    )
    power = jnp.mean(whole * whole, axis=1, keepdims=True)
    normed = (whole * lax.rsqrt(power + EPS) * norm_gains[0][None, :]).astype(jnp.bfloat16)
    state = lax.dynamic_slice_in_dim(whole, column, local, 1)
    qkv = jnp.einsum("ld,kde->kle", normed, self_qkv, preferred_element_type=jnp.float32).astype(
        jnp.bfloat16
    )
    self_q = qkv[0].reshape(lat_rows, nheads, HEAD)
    self_k = qkv[1].reshape(lat_rows, nheads, HEAD)
    self_v = qkv[2].reshape(lat_rows, nheads, HEAD)
    inner = jnp.einsum("lhc,mhc->hlm", self_q, self_k, preferred_element_type=jnp.float32) * scale
    raised = jnp.exp(inner)
    probs = (raised / jnp.sum(raised, axis=2, keepdims=True)).astype(jnp.bfloat16)
    head_out = (
        jnp.einsum("hlm,mhc->lhc", probs, self_v, preferred_element_type=jnp.float32)
        .astype(jnp.bfloat16)
        .reshape(lat_rows, local)
    )
    every_head = ring_gather(head_out.T, "heads", n_heads).T
    out_whole = whole + jnp.dot(every_head, out_full, preferred_element_type=jnp.float32)
    latents_out = lax.dynamic_slice_in_dim(out_whole, column, local, 1)
    power_two = jnp.mean(out_whole * out_whole, axis=1, keepdims=True)
    normed2 = (out_whole * lax.rsqrt(power_two + EPS) * norm_gains[1][None, :]).astype(jnp.bfloat16)
    dec = jnp.einsum("ld,kde->kle", normed2, dec_kv, preferred_element_type=jnp.float32).astype(
        jnp.bfloat16
    )
    dec_keys = dec[0].reshape(lat_rows, nheads, HEAD)
    dec_vals = dec[1].reshape(lat_rows, nheads, HEAD)
    query = jnp.dot(enc, dq_full, preferred_element_type=jnp.float32).astype(jnp.bfloat16)
    dec_q = query.reshape(count, nheads, HEAD)
    logits = jnp.einsum("thc,lhc->htl", dec_q, dec_keys, preferred_element_type=jnp.float32) * scale
    lifted = jnp.exp(logits)
    weights = lifted / jnp.sum(lifted, axis=2, keepdims=True)
    out = jnp.einsum(
        "htl,lhc->thc", weights.astype(jnp.bfloat16), dec_vals, preferred_element_type=jnp.float32
    )
    read = readout.reshape(nheads, HEAD)
    onehot = (horizon_ids[:, None] == jnp.arange(HORIZONS, dtype=jnp.int32)[None, :]).astype(
        jnp.float32
    )
    target = jnp.sum(onehot * horizon_levels[None, :], axis=1)
    value_read = jnp.einsum("lhc,hc->hl", dec_vals.astype(jnp.float32), read, precision=high)
    lever = (
        weights
        * (
            value_read[:, None, :]
            - jnp.sum(value_read[:, None, :] * weights, axis=2, keepdims=True)
        )
    ).astype(jnp.bfloat16)
    pull = jnp.einsum("htl,lhc->thc", lever, dec_keys, preferred_element_type=jnp.float32) * scale
    field = pair_sum(jnp.sum(out * read[None, :, :], axis=(1, 2)), "heads", n_heads)
    miss = field - target
    dquery = (miss[:, None, None] * pull).reshape(count, local).astype(jnp.bfloat16)
    grad_query = lax.psum_scatter(
        jnp.dot(enc.T, dquery, preferred_element_type=jnp.float32).astype(jnp.bfloat16),
        "picks",
        scatter_dimension=0,
        tiled=True,
    ).astype(jnp.float32)
    return (field, latents_out, grad_query)


def solution(mesh):
    in_specs = (
        P(None, ("groups", "picks")),
        P(("groups", "picks")),
        P("groups"),
        P(),
        P("picks", None, "heads"),
        P("heads", None),
        P(),
        P(None, None, "heads"),
        P(None, "heads"),
        P(None, None, "heads"),
        P("picks", "heads"),
        P("heads"),
    )
    out_specs = (P(("groups", "picks")), P("groups", "heads"), P(("groups", "picks"), "heads"))
    body = functools.partial(
        on_device,
        n_picks=mesh.shape["picks"],
        n_heads=mesh.shape["heads"],
        n_groups=mesh.shape["groups"],
    )
    return jax.shard_map(body, mesh=mesh, in_specs=in_specs, out_specs=out_specs, check_vma=False)
```

profile of v0, /device:TPU:0, one launch (start us, length us, event | category | flops | bytes accessed | tf_op | source)
XLA Modules:
  0.0 216.1 jit_solution(17237952158772773728)
XLA Ops:
  7.2 0.7 all-gather.6.cloned.1.call-update
  8.0 1.2 copy.60
  9.2 2.4 %collective-permute-start = (bf16[256,1024]{1,0:T(8,128)(2,1)S(1)}, bf16[256,1024]{1,0:T(8,128)(2,1)S(1)}, u32[]{:S(2)}, u32[]{:S(2)}) collective-permute-start(bf16[256,1024]{1,0:T(8,128)(2,1)S(1)} %bitcast.124), channel_id=1, source_target_pairs={{0,3},{1,0},{2,1},{3,2},{4,7},{5,4},{6,5},{7,6},{8,11},{9,8},{10,9... | collective-permute-start | bytes 1572872 | tf_op jit(solution)/shard_map/ppermute | solution.py:30
  11.7 0.6 collective-permute-start.1
  12.4 1.7 collective-permute-start.4
  14.1 1.0 constant_dynamic-slice_fusion.1
  15.1 0.1 copy.97
  15.2 0.1 maximum_multiply_fusion
  15.3 22.8 %fusion = (bf16[3,512,1024]{2,1,0:T(8,128)(2,1)S(1)}, bf16[3,512,1024]{2,1,0:T(8,128)(2,1)S(1)}) fusion(f32[3,1024]{1,0:T(4,128)S(1)} %copy-done.9, f32[512]{0:T(512)S(1)} %maximum_multiply_fusion), kind=kLoop, calls=%fused_computation.2 | loop fusion | flops 4718592 | bytes 6305792 | tf_op jit(solution)/shard_map/convert
  38.2 3.2 %pad_maximum_fusion = bf16[6,512,1024]{2,1,0:T(8,128)(2,1)} fusion(bf16[3,512,1024]{2,1,0:T(8,128)(2,1)S(1)} %get-tuple-element.29, bf16[3,512,1024]{2,1,0:T(8,128)(2,1)S(1)} %get-tuple-element.28), kind=kLoop, calls=%fused_computation.4 | loop fusion | flops 3145728 | bytes 12582912 | tf_op jit(solution)/shard_map/concatenate | solution.py:18
  41.4 5.1 %collective-permute-done.3 = bf16[256,1024]{1,0:T(8,128)(2,1)} collective-permute-done((bf16[256,1024]{1,0:T(8,128)(2,1)}, bf16[256,1024]{1,0:T(8,128)(2,1)}, u32[]{:S(2)}, u32[]{:S(2)}) %collective-permute-start.3) | collective-permute-done | bytes 524320 | tf_op jit(solution)/shard_map/ppermute | solution.py:30
  46.4 1.1 collective-permute-start.2
  47.5 8.8 %collective-permute-done.4 = bf16[256,1024]{1,0:T(8,128)(2,1)} collective-permute-done((bf16[256,1024]{1,0:T(8,128)(2,1)}, bf16[256,1024]{1,0:T(8,128)(2,1)}, u32[]{:S(2)}, u32[]{:S(2)}) %collective-permute-start.4) | collective-permute-done | bytes 524320 | tf_op jit(solution)/shard_map/ppermute | solution.py:30
  56.3 5.1 %fusion.14 = bf16[4,256,1024]{2,1,0:T(8,128)(2,1)} fusion(s32[]{:T(128)S(6)} %select_n.27, bf16[1,256,1024]{2,1,0:T(8,128)(2,1)S(1)} %bitcast.143, bf16[1,256,1024]{2,1,0:T(8,128)(2,1)} %bitcast.13, bf16[1,256,1024]{2,1,0:T(8,128)(2,1)} %bitcast.14, bf16[1,256,1024]{2,1,0:T(8,128)(2,1)} %bitcast.15), kind=kLoop, calls=%fused_computation.38 | loop fusion | flops 7340032 | bytes 4194308 | tf_op jit(solution)/shard_map/jit(_roll_dynamic)/concatenate | solution.py:32
  61.4 14.5 %all-gather.6.cloned.1.call-done = bf16[3072,2,256]{2,1,0:T(2,128)(2,1)} async-done(((bf16[768,2,256]{2,1,0:T(2,128)(2,1)}), bf16[3072,2,256]{2,1,0:T(2,128)(2,1)}) %all-gather.6.cloned.1.call-update) | async-done | bytes 3145744 | tf_op jit(solution)/shard_map/all_gather | solution.py:89
  75.8 7.1 %fusion.32 = bf16[1024,2,256]{0,2,1:T(8,128)(2,1)S(1)} fusion(bf16[3072,1024,1]{1,0,2:T(8,128)(2,1)} %bitcast.118, bf16[3072,2,256]{2,1,0:T(2,128)(2,1)} %all-gather.6.cloned.1.call-done), kind=kOutput, calls=%fused_computation.81 | convolution fusion | flops 3221749760 | bytes 10485760 | tf_op jit(solution)/shard_map/tf,fjc->tjc/dot_general | solution.py:91
  83.0 0.1 fusion.78
  83.1 0.8 multiply_reduce_fusion.1
  83.9 2.0 copy-done.1
  86.0 1.6 fusion.43
  87.6 0.2 all-gather.8.cloned.1.call-start
  87.9 4.8 %fusion.21 = bf16[4,256,1024]{2,1,0:T(8,128)(2,1)} fusion(s32[]{:T(128)S(6)} %select_n.27, bf16[1,256,1024]{2,1,0:T(8,128)(2,1)S(1)} %bitcast.127, bf16[1,256,1024]{2,1,0:T(8,128)(2,1)S(1)} %bitcast.144, bf16[1,256,1024]{2,1,0:T(8,128)(2,1)} %bitcast.5, bf16[1,256,1024]{2,1,0:T(8,128)(2,1)} %bitcast.6), kind=kLoop, calls=%fused_computation.45 | loop fusion | flops 7340032 | bytes 4194308 | tf_op jit(solution)/shard_map/jit(_roll_dynamic)/concatenate | solution.py:32
  92.6 0.9 fusion.4
  93.6 13.3 %all-gather.1 = f32[8,2,512]{2,1,0:T(2,128)S(1)} all-gather(f32[2,2,512]{2,1,0:T(2,128)S(1)} %pad_maximum_fusion.1), channel_id=3, replica_groups=mesh['groups'=2,'picks'=4,'heads'=4] {'picks'}, dimensions={0}, use_global_device_ids=true | all-gather | bytes 40960 | tf_op jit(solution)/shard_map/all_gather | solution.py:105
  106.9 7.8 %all-gather.10.cloned.1.call-done = bf16[8,512,128]{2,1,0:T(8,128)(2,1)} async-done(((bf16[2,512,128]{2,1,0:T(8,128)(2,1)}), bf16[8,512,128]{2,1,0:T(8,128)(2,1)}) %all-gather.10.cloned.1.call-update) | async-done | bytes 1048592 | tf_op jit(solution)/shard_map/all_gather | solution.py:104
  114.7 1.8 multiply_reduce_fusion.2
  116.5 0.2 copy.85
  116.7 0.9 collective-permute-start.6
  117.6 0.7 collective-permute-start.7
  118.3 0.2 collective-permute-start.8
  118.6 5.6 %collective-permute-done.6 = bf16[256,512]{1,0:T(8,128)(2,1)S(1)} collective-permute-done((bf16[256,512]{1,0:T(8,128)(2,1)S(1)}, bf16[256,512]{1,0:T(8,128)(2,1)S(1)}, u32[]{:S(2)}, u32[]{:S(2)}) %collective-permute-start.6) | collective-permute-done | bytes 262176 | tf_op jit(solution)/shard_map/ppermute | solution.py:30
  124.2 6.7 %collective-permute-done.7 = bf16[256,512]{1,0:T(8,128)(2,1)S(1)} collective-permute-done((bf16[256,512]{1,0:T(8,128)(2,1)S(1)}, bf16[256,512]{1,0:T(8,128)(2,1)S(1)}, u32[]{:S(2)}, u32[]{:S(2)}) %collective-permute-start.7) | collective-permute-done | bytes 262176 | tf_op jit(solution)/shard_map/ppermute | solution.py:30
  130.9 0.2 collective-permute-done.8
  131.1 2.2 %fusion.60 = bf16[4,256,512]{2,1,0:T(8,128)(2,1)S(1)} fusion(s32[]{:T(128)S(6)} %select_n.27, bf16[1,256,512]{2,1,0:T(8,128)(2,1)S(1)} %bitcast.133, bf16[1,256,512]{2,1,0:T(8,128)(2,1)S(1)} %bitcast.147, bf16[1,256,512]{2,1,0:T(8,128)(2,1)S(1)} %bitcast.148, bf16[1,256,512]{2,1,0:T(8,128)(2,1)} %bitcast.32), kind=kLoop, calls=%fused_computation.103 | loop fusion | flops 3670016 | bytes 2097156 | tf_op jit(solution)/shard_map/jit(_roll_dynamic)/concatenate | solution.py:32
  133.4 1.4 multiply_reduce_fusion.4
  134.8 1.1 fusion.38
  136.0 0.5 fusion.31
  136.5 0.5 convolution_convert_fusion.4
  137.1 1.5 collective-permute-start.10
  138.6 0.2 collective-permute-start.11
  138.8 0.1 select_reduce_fusion
  138.9 4.0 %collective-permute-done.9 = bf16[256,512]{1,0:T(8,128)(2,1)S(1)} collective-permute-done((bf16[256,512]{1,0:T(8,128)(2,1)S(1)}, bf16[256,512]{1,0:T(8,128)(2,1)S(1)}, u32[]{:S(2)}, u32[]{:S(2)}) %collective-permute-start.9) | collective-permute-done | bytes 262176 | tf_op jit(solution)/shard_map/ppermute | solution.py:30
  142.9 8.3 %collective-permute-done.10 = bf16[256,512]{1,0:T(8,128)(2,1)S(1)} collective-permute-done((bf16[256,512]{1,0:T(8,128)(2,1)S(1)}, bf16[256,512]{1,0:T(8,128)(2,1)S(1)}, u32[]{:S(2)}, u32[]{:S(2)}) %collective-permute-start.10) | collective-permute-done | bytes 262176 | tf_op jit(solution)/shard_map/ppermute | solution.py:30
  151.1 0.2 collective-permute-done.11
  151.3 1.2 fusion.53
  152.6 1.4 multiply_reduce_fusion.3
  154.0 1.3 copy-done.4
  155.3 0.8 fusion.42
  156.3 5.1 %convolution_convert_fusion.2 = bf16[1024,256]{0,1:T(8,128)(2,1)S(1)} fusion(bf16[3072,1024]{1,0:T(8,128)(2,1)} %bitcast.119, bf16[3072,256]{1,0:T(8,128)(2,1)} %all-gather.8.cloned.1.call-done), kind=kOutput, calls=%fused_computation.84 | convolution fusion | flops 1610874880 | bytes 8388608 | tf_op jit(solution)/shard_map/dot_general | solution.py:153
  161.3 0.8 fusion.3
  162.2 1.0 fusion.39
  163.2 0.1 collective-permute-start.12
  163.2 0.2 fusion.82
  163.4 0.9 collective-permute-done.12
  164.4 0.9 collective-permute-start.13
  165.3 0.9 multiply_reduce_fusion
  166.1 1.9 collective-permute-done.13
  168.0 0.6 subtract_multiply_fusion
  168.6 1.2 multiply_convert_fusion.4
  169.9 0.3 slice-done.1
  170.2 3.1 %convolution_convert_fusion = bf16[3072,256]{1,0:T(8,128)(2,1)} fusion(bf16[3072,1024]{1,0:T(8,128)(2,1)S(1)} %bitcast.122, bf16[1024,256]{0,1:T(8,128)(2,1)S(1)} %bitcast.168), kind=kOutput, calls=%fused_computation.26 | convolution fusion | flops 1611399168 | bytes 8388608 | tf_op jit(solution)/shard_map/dot_general | solution.py:179
  173.4 1.9 constant_dynamic-slice_fusion
  175.2 32.4 %reduce-scatter.2.cloned.1.call-done = bf16[768,256]{1,0:T(8,128)(2,1)} async-done(((bf16[3072,256]{1,0:T(8,128)(2,1)}), bf16[768,256]{1,0:T(8,128)(2,1)}) %reduce-scatter.2.cloned.1.call-update) | async-done | bytes 393232 | tf_op jit(solution)/shard_map/reduce_scatter | solution.py:178
  207.6 1.9 convert_element_type.100
  (56 shorter events, 0.6 us)
Async XLA Ops:
  7.2 127.6 %copy-start = (bf16[3,1024,256]{2,1,0:T(8,128)(2,1)S(1)}, bf16[3,1024,256]{2,1,0:T(8,128)(2,1)}, u32[]{:S(2)}) copy-start(bf16[3,1024,256]{2,1,0:T(8,128)(2,1)} %param.23) | copy-start | bytes 4718596
  7.2 8.1 %copy-start.9 = (f32[3,1024]{1,0:T(4,128)S(1)}, f32[3,1024]{1,0:T(4,128)}, u32[]{:S(2)}) copy-start(f32[3,1024]{1,0:T(4,128)} %param.16) | copy-start | bytes 36868
  7.2 68.7 %all-gather.6.cloned.1.call-start = ((), (), s32[]{:S(2)}) async-start(), calls=%async_computation.1 | async-start | bytes 3932160 | tf_op jit(solution)/shard_map/all_gather | solution.py:89
  7.9 106.8 %all-gather.10.cloned.1.call-start = ((), (), s32[]{:S(2)}) async-start(), calls=%async_computation.4 | async-start | bytes 1310720 | tf_op jit(solution)/shard_map/all_gather | solution.py:104
  9.2 78.6 %collective-permute-start = (bf16[256,1024]{1,0:T(8,128)(2,1)S(1)}, bf16[256,1024]{1,0:T(8,128)(2,1)S(1)}, u32[]{:S(2)}, u32[]{:S(2)}) collective-permute-start(bf16[256,1024]{1,0:T(8,128)(2,1)S(1)} %bitcast.124), channel_id=1, source_target_pairs={{0,3},{1,0},{2,1},{3,2},{4,7},{5,4},{6,5},{7,6},{8,11},{9,8},{10,9... | collective-permute-start | bytes 1572872 | tf_op jit(solution)/shard_map/ppermute | solution.py:30
  11.7 76.2 %collective-permute-start.1 = (bf16[256,1024]{1,0:T(8,128)(2,1)S(1)}, bf16[256,1024]{1,0:T(8,128)(2,1)}, u32[]{:S(2)}, u32[]{:S(2)}) collective-permute-start(bf16[256,1024]{1,0:T(8,128)(2,1)S(1)} %bitcast.125), channel_id=1, source_target_pairs={{0,2},{1,3},{2,0},{3,1},{4,6},{5,7},{6,4},{7,5},{8,10},{9,11},{10,... | collective-permute-start | bytes 1572872 | tf_op jit(solution)/shard_map/ppermute | solution.py:30
  12.3 34.1 %collective-permute-start.3 = (bf16[256,1024]{1,0:T(8,128)(2,1)}, bf16[256,1024]{1,0:T(8,128)(2,1)}, u32[]{:S(2)}, u32[]{:S(2)}) collective-permute-start(bf16[256,1024]{1,0:T(8,128)(2,1)} %param.21), channel_id=1, source_target_pairs={{0,3},{1,0},{2,1},{3,2},{4,7},{5,4},{6,5},{7,6},{8,11},{9,8},{10,9... | collective-permute-start | bytes 1572872 | tf_op jit(solution)/shard_map/ppermute | solution.py:30
  12.4 43.9 %collective-permute-start.4 = (bf16[256,1024]{1,0:T(8,128)(2,1)}, bf16[256,1024]{1,0:T(8,128)(2,1)}, u32[]{:S(2)}, u32[]{:S(2)}) collective-permute-start(bf16[256,1024]{1,0:T(8,128)(2,1)} %param.21), channel_id=1, source_target_pairs={{0,2},{1,3},{2,0},{3,1},{4,6},{5,7},{6,4},{7,5},{8,10},{9,11},{10,... | collective-permute-start | bytes 1572872 | tf_op jit(solution)/shard_map/ppermute | solution.py:30
  14.1 42.2 %collective-permute-start.5 = (bf16[256,1024]{1,0:T(8,128)(2,1)}, bf16[256,1024]{1,0:T(8,128)(2,1)}, u32[]{:S(2)}, u32[]{:S(2)}) collective-permute-start(bf16[256,1024]{1,0:T(8,128)(2,1)} %param.21), channel_id=1, source_target_pairs={{0,1},{1,2},{2,3},{3,0},{4,5},{5,6},{6,7},{7,4},{8,9},{9,10},{10,1... | collective-permute-start | bytes 1572872 | tf_op jit(solution)/shard_map/ppermute | solution.py:30
  38.2 18.1 %copy-start.8 = (bf16[256,1024]{1,0:T(8,128)(2,1)S(1)}, bf16[256,1024]{1,0:T(8,128)(2,1)}, u32[]{:S(2)}) copy-start(bf16[256,1024]{1,0:T(8,128)(2,1)} %param.21) | copy-start | bytes 1572868
  46.4 41.4 %collective-permute-start.2 = (bf16[256,1024]{1,0:T(8,128)(2,1)S(1)}, bf16[256,1024]{1,0:T(8,128)(2,1)}, u32[]{:S(2)}, u32[]{:S(2)}) collective-permute-start(bf16[256,1024]{1,0:T(8,128)(2,1)S(1)} %bitcast.126), channel_id=1, source_target_pairs={{0,1},{1,2},{2,3},{3,0},{4,5},{5,6},{6,7},{7,4},{8,9},{9,10},{10,1... | collective-permute-start | bytes 1572872 | tf_op jit(solution)/shard_map/ppermute | solution.py:30
  83.9 2.0 copy-start.1
  87.6 68.7 %all-gather.8.cloned.1.call-start = ((), (), s32[]{:S(2)}) async-start(), calls=%async_computation.2 | async-start | bytes 1966080 | tf_op jit(solution)/shard_map/all_gather | solution.py:121
  87.8 4.8 %copy-start.2 = (f32[2,512,1024]{2,1,0:T(8,128)S(1)}, f32[2,512,1024]{2,1,0:T(8,128)}, u32[]{:S(2)}) copy-start(f32[2,512,1024]{2,1,0:T(8,128)} %copy-done.1) | copy-start | bytes 12582916
  93.5 24.9 %copy-start.10 = (f32[2,1024]{1,0:T(2,128)S(1)}, f32[2,1024]{1,0:T(2,128)}, u32[]{:S(2)}) copy-start(f32[2,1024]{1,0:T(2,128)} %param.22) | copy-start | bytes 24580
  116.7 16.7 %copy-start.6 = (bf16[512,1024]{1,0:T(8,128)(2,1)S(1)}, bf16[512,1024]{1,0:T(8,128)(2,1)}, u32[]{:S(2)}) copy-start(bf16[512,1024]{1,0:T(8,128)(2,1)} %param.19) | copy-start | bytes 3145732
  116.7 7.5 %collective-permute-start.6 = (bf16[256,512]{1,0:T(8,128)(2,1)S(1)}, bf16[256,512]{1,0:T(8,128)(2,1)S(1)}, u32[]{:S(2)}, u32[]{:S(2)}) collective-permute-start(bf16[256,512]{1,0:T(8,128)(2,1)S(1)} %bitcast.130), channel_id=1, source_target_pairs={{0,3},{1,0},{2,1},{3,2},{4,7},{5,4},{6,5},{7,6},{8,11},{9,8},{10,9... | collective-permute-start | bytes 786440 | tf_op jit(solution)/shard_map/ppermute | solution.py:30
  117.6 13.3 %collective-permute-start.7 = (bf16[256,512]{1,0:T(8,128)(2,1)S(1)}, bf16[256,512]{1,0:T(8,128)(2,1)S(1)}, u32[]{:S(2)}, u32[]{:S(2)}) collective-permute-start(bf16[256,512]{1,0:T(8,128)(2,1)S(1)} %bitcast.131), channel_id=1, source_target_pairs={{0,2},{1,3},{2,0},{3,1},{4,6},{5,7},{6,4},{7,5},{8,10},{9,11},{10,... | collective-permute-start | bytes 786440 | tf_op jit(solution)/shard_map/ppermute | solution.py:30
  118.3 12.8 %collective-permute-start.8 = (bf16[256,512]{1,0:T(8,128)(2,1)S(1)}, bf16[256,512]{1,0:T(8,128)(2,1)}, u32[]{:S(2)}, u32[]{:S(2)}) collective-permute-start(bf16[256,512]{1,0:T(8,128)(2,1)S(1)} %bitcast.132), channel_id=1, source_target_pairs={{0,1},{1,2},{2,3},{3,0},{4,5},{5,6},{6,7},{7,4},{8,9},{9,10},{10,1... | collective-permute-start | bytes 786440 | tf_op jit(solution)/shard_map/ppermute | solution.py:30
  118.5 89.1 %reduce-scatter.2.cloned.1.call-start = ((), (), s32[]{:S(2)}) async-start(), calls=%async_computation.3 | async-start | bytes 1966080 | tf_op jit(solution)/shard_map/reduce_scatter | solution.py:178
  118.6 14.8 %copy-start.3 = (bf16[4,256,1024]{2,1,0:T(8,128)(2,1)S(1)}, bf16[4,256,1024]{2,1,0:T(8,128)(2,1)}, u32[]{:S(2)}) copy-start(bf16[4,256,1024]{2,1,0:T(8,128)(2,1)} %fusion.14) | copy-start | bytes 6291460
  136.5 2.3 %copy-start.11 = (s32[1024]{0:T(1024)S(1)}, s32[1024]{0:T(1024)}, u32[]{:S(2)}) copy-start(s32[1024]{0:T(1024)} %param.17) | copy-start | bytes 12292
  136.5 2.3 %copy-start.13 = (f32[64]{0:T(128)S(1)}, f32[64]{0:T(128)}, u32[]{:S(2)}) copy-start(f32[64]{0:T(128)} %param.18) | copy-start | bytes 772
  137.1 15.5 %copy-start.5 = (bf16[4,256,1024]{2,1,0:T(8,128)(2,1)S(1)}, bf16[4,256,1024]{2,1,0:T(8,128)(2,1)}, u32[]{:S(2)}) copy-start(bf16[4,256,1024]{2,1,0:T(8,128)(2,1)} %fusion.21) | copy-start | bytes 6291460
  137.1 5.8 %collective-permute-start.9 = (bf16[256,512]{1,0:T(8,128)(2,1)S(1)}, bf16[256,512]{1,0:T(8,128)(2,1)S(1)}, u32[]{:S(2)}, u32[]{:S(2)}) collective-permute-start(bf16[256,512]{1,0:T(8,128)(2,1)S(1)} %bitcast.149), channel_id=1, source_target_pairs={{0,3},{1,0},{2,1},{3,2},{4,7},{5,4},{6,5},{7,6},{8,11},{9,8},{10,9... | collective-permute-start | bytes 786440 | tf_op jit(solution)/shard_map/ppermute | solution.py:30
  137.1 14.0 %collective-permute-start.10 = (bf16[256,512]{1,0:T(8,128)(2,1)S(1)}, bf16[256,512]{1,0:T(8,128)(2,1)S(1)}, u32[]{:S(2)}, u32[]{:S(2)}) collective-permute-start(bf16[256,512]{1,0:T(8,128)(2,1)S(1)} %bitcast.150), channel_id=1, source_target_pairs={{0,2},{1,3},{2,0},{3,1},{4,6},{5,7},{6,4},{7,5},{8,10},{9,11},{10,... | collective-permute-start | bytes 786440 | tf_op jit(solution)/shard_map/ppermute | solution.py:30
  138.6 12.7 %collective-permute-start.11 = (bf16[256,512]{1,0:T(8,128)(2,1)S(1)}, bf16[256,512]{1,0:T(8,128)(2,1)S(1)}, u32[]{:S(2)}, u32[]{:S(2)}) collective-permute-start(bf16[256,512]{1,0:T(8,128)(2,1)S(1)} %bitcast.151), channel_id=1, source_target_pairs={{0,1},{1,2},{2,3},{3,0},{4,5},{5,6},{6,7},{7,4},{8,9},{9,10},{10,1... | collective-permute-start | bytes 786440 | tf_op jit(solution)/shard_map/ppermute | solution.py:30
  152.6 2.8 %copy-start.7 = (bf16[2,1024,256]{2,1,0:T(8,128)(2,1)S(1)}, bf16[2,1024,256]{2,1,0:T(8,128)(2,1)}, u32[]{:S(2)}) copy-start(bf16[2,1024,256]{2,1,0:T(8,128)(2,1)} %param.25) | copy-start | bytes 3145732
  154.0 1.4 copy-start.4
  161.3 0.9 copy-start.12
  163.2 1.2 collective-permute-start.12
  164.4 3.6 %collective-permute-start.13 = (f32[1024]{0:T(1024)S(1)}, f32[1024]{0:T(1024)S(1)}, u32[]{:S(2)}, u32[]{:S(2)}) collective-permute-start(f32[1024]{0:T(1024)S(1)} %add.61), channel_id=1, source_target_pairs={{0,2},{1,3},{2,0},{3,1},{4,6},{5,7},{6,4},{7,5},{8,10},{9,11},{10,... | collective-permute-start | bytes 12296 | tf_op jit(solution)/shard_map/ppermute | solution.py:58
  165.3 4.6 %slice-start = ((s8[6291456]{0:T(1024)(128)(4,1)}), s8[4194304]{0:T(1024)(128)(4,1)S(1)}, s32[]{:S(2)}) async-start(s8[6291456]{0:T(1024)(128)(4,1)} %bitcast.120), calls=%async_computation.5 | async-start | bytes 8388608
  168.6 1.6 slice-start.1
Sparse Core Ops, SparseCore 0:
  9.6 66.2 all-gather.5
  87.7 26.9 all-gather.9
  118.7 36.9 all-gather.7
  173.5 34.0 reduce-scatter.1
where the time goes:
time: 216 us
  waiting for transfers between devices  97 us (45%)
  other arithmetic  45.7 us (21%)
  matrix products  26.8 us (12%)
  between operations  14.2 us (7%)
  blocking collectives  13.3 us (6%)
  starting transfers between devices  10.7 us (5%)
  local copies, waits for them, and re-layouts  8.39 us (4%)
    ppermute x12, waiting for transfers between devices, ring_gather(): blocks.append(lax.ppermute(x, axis, [(i, (i - s) % n) for i in range(n)]))  38.8 us
    reduce_scatter x1, waiting for transfers between devices, on_device(): lax.psum_scatter(jnp.dot(enc.T, dquery, preferred_element_type=jnp.float3...  32.4 us
    another operation x1, other arithmetic  22.8 us
    all_gather x1, waiting for transfers between devices, on_device(): piece = lax.all_gather(kv_weight, 'picks', axis=0, tiled=True)  14.5 us
    concatenate x4, other arithmetic, ring_gather(): ordered = jnp.roll(flipped, idx, axis=0)  13.3 us
    all_gather x1, blocking collectives, on_device(): lax.all_gather(jnp.stack([top, total]), 'picks', axis=0, tiled=False)  13.3 us
    ppermute x12, starting transfers between devices, ring_gather(): blocks.append(lax.ppermute(x, axis, [(i, (i - s) % n) for i in range(n)]))  9.4 us
    all_gather x1, waiting for transfers between devices, on_device(): lax.all_gather(numer.astype(jnp.bfloat16), 'picks', axis=0, tiled=False)  7.77 us
  transfers between devices with their start and end apart: 18, of which 13 were waited for; matrix products, arithmetic and copies ran while one was open for 28% of the time, Pallas kernels for 0%

commit v1 on v0

--- a/solution.py
+++ b/solution.py
@@ -10,6 +10,16 @@
 PI = 3.141592653589793
 EPS = 1e-06
 RING_MAX = 4
+
+
+def ring_gather_2(x, axis, dim):
+    ways, here, step = (lax.axis_size(axis), lax.axis_index(axis), x.shape[dim])
+    shape = [n * ways if d == dim else n for d, n in enumerate(x.shape)]
+    full = lax.dynamic_update_slice_in_dim(jnp.zeros(shape, x.dtype), x, here * step, axis=dim)
+    for far in range(1, ways):
+        x = lax.ppermute(x, axis, [(d, (d + 1) % ways) for d in range(ways)])
+        full = lax.dynamic_update_slice_in_dim(full, x, (here - far) % ways * step, axis=dim)
+    return full
 
 
 def encode(coords):
@@ -86,7 +96,7 @@
     column = lax.axis_index("heads") * local
     enc = encode(coords)
     cross_full = ring_gather(cross_out, "heads", n_heads)
-    piece = lax.all_gather(kv_weight, "picks", axis=0, tiled=True)
+    piece = ring_gather_2(kv_weight, "picks", 0)
     cross_full, piece = lax.optimization_barrier((cross_full, piece))
     keys_vals = jnp.einsum("tf,fjc->tjc", enc, piece, preferred_element_type=jnp.float32).astype(
         jnp.bfloat16

time: 216 us -> 232 us (1.074)
  local copies, waits for them, and re-layouts: 8.39 us -> 23.3 us
  waiting for transfers between devices: 97 us -> 90.3 us
  starting transfers between devices: 10.7 us -> 13.7 us
  other arithmetic: 45.7 us -> 48.6 us
    ppermute x0 -> x3, waiting for transfers between devices: none -> 22.6 us  [ring_gather_2(): x = lax.ppermute(x, axis, [(d, (d + 1) % ways) for d in range(ways)])]
    all_gather x1 -> x0, waiting for transfers between devices: 14.5 us -> none  [on_device(): piece = lax.all_gather(kv_weight, 'picks', axis=0, tiled=True)]
    ppermute x12, waiting for transfers between devices: 38.8 us -> 24.9 us  [ring_gather(): blocks.append(lax.ppermute(x, axis, [(i, (i - s) % n) for i in range(n)]))]
    ppermute x0 -> x3, local copies, waits for them, and re-layouts: none -> 6.68 us  [ring_gather_2(): x = lax.ppermute(x, axis, [(d, (d + 1) % ways) for d in range(ways)])]
    unnamed x34 -> x39, local copies, waits for them, and re-layouts: 5.17 us -> 9.87 us
    ppermute x0 -> x3, starting transfers between devices: none -> 4.42 us  [ring_gather_2(): x = lax.ppermute(x, axis, [(d, (d + 1) % ways) for d in range(ways)])]
    dynamic_update_slice x0 -> x4, local copies, waits for them, and re-layouts: none -> 3.18 us  [the longest x3 3.08 us: ring_gather_2(): lax.dynamic_update_slice_in_dim(full, x, (here - far) % ways * step, axis...]
  transfers between devices with their start and end apart: 18 -> 20, of which waited for: 13 -> 12; matrix products, arithmetic and copies ran while one was open for 28% -> 34% of each run, Pallas kernels for 0% -> 0%
where the time goes in v1:
time: 232 us; the launch traced here: 231 us
  waiting for transfers between devices  90.3 us (39%)
  other arithmetic  48.6 us (21%)
  matrix products  28 us (12%)
  local copies, waits for them, and re-layouts  23.3 us (10%)
  between operations  14.2 us (6%)
  starting transfers between devices  13.7 us (6%)
  blocking collectives  13.2 us (6%)
    reduce_scatter x1, waiting for transfers between devices, on_device(): lax.psum_scatter(jnp.dot(enc.T, dquery, preferred_element_type=jnp.float3...  32.4 us
    ppermute x12, waiting for transfers between devices, ring_gather(): blocks.append(lax.ppermute(x, axis, [(i, (i - s) % n) for i in range(n)]))  24.9 us
    another operation x1, other arithmetic  24.5 us
    ppermute x3, waiting for transfers between devices, ring_gather_2(): x = lax.ppermute(x, axis, [(d, (d + 1) % ways) for d in range(ways)])  22.6 us
    all_gather x1, blocking collectives, on_device(): lax.all_gather(jnp.stack([top, total]), 'picks', axis=0, tiled=False)  13.2 us
    concatenate x4, other arithmetic, ring_gather(): ordered = jnp.roll(flipped, idx, axis=0)  12.6 us
    unnamed x39, local copies, waits for them, and re-layouts  9.87 us
    ppermute x12, starting transfers between devices, ring_gather(): blocks.append(lax.ppermute(x, axis, [(i, (i - s) % n) for i in range(n)]))  8.17 us
  transfers between devices with their start and end apart: 20, of which 12 were waited for; matrix products, arithmetic and copies ran while one was open for 34% of the time, Pallas kernels for 0%

profile of v1, /device:TPU:0, one launch (start us, length us, event | category | flops | bytes accessed | tf_op | source)
XLA Modules:
  0.0 231.4 jit_solution(8625089884025920528)
XLA Ops:
  7.2 3.1 %collective-permute-start.6 = (bf16[768,2,256]{2,1,0:T(2,128)(2,1)}, bf16[768,2,256]{2,1,0:T(2,128)(2,1)}, u32[]{:S(2)}, u32[]{:S(2)}) collective-permute-start(bf16[768,2,256]{2,1,0:T(2,128)(2,1)} %param.20), channel_id=1, source_target_pairs={{0,4},{4,8},{8,12},{12,0},{1,5},{5,9},{9,13},{13,1},{2,6},{6,10},{... | collective-permute-start | bytes 2359304 | tf_op jit(solution)/shard_map/ppermute | solution.py:20
  10.3 0.7 collective-permute-start.3
  11.0 0.8 collective-permute-start.4
  11.8 0.2 collective-permute-start.5
  12.0 1.2 copy.69
  13.3 1.6 collective-permute-start
  14.9 2.2 copy.71
  17.2 13.0 %collective-permute-done.6 = bf16[768,2,256]{2,1,0:T(2,128)(2,1)} collective-permute-done((bf16[768,2,256]{2,1,0:T(2,128)(2,1)}, bf16[768,2,256]{2,1,0:T(2,128)(2,1)}, u32[]{:S(2)}, u32[]{:S(2)}) %collective-permute-start.6) | collective-permute-done | bytes 786464 | tf_op jit(solution)/shard_map/ppermute | solution.py:20
  30.2 24.5 %fusion = (bf16[3,512,1024]{2,1,0:T(8,128)(2,1)}, bf16[3,512,1024]{2,1,0:T(8,128)(2,1)}) fusion(f32[3,1024]{1,0:T(4,128)S(1)} %copy-done.11, f32[512]{0:T(512)S(1)} %maximum_multiply_fusion), kind=kLoop, calls=%fused_computation.2 | loop fusion | flops 4718592 | bytes 6305792 | tf_op jit(solution)/shard_map/convert
  54.7 1.0 constant_dynamic-slice_fusion.1
  55.8 0.4 broadcast_in_dim.4
  56.3 2.5 %copy-done.4 = bf16[3,512,1024]{2,1,0:T(8,128)(2,1)S(1)} copy-done((bf16[3,512,1024]{2,1,0:T(8,128)(2,1)S(1)}, bf16[3,512,1024]{2,1,0:T(8,128)(2,1)}, u32[]{:S(2)}) %copy-start.4) | copy-done | bytes 3145752
  58.8 5.2 %pad_maximum_fusion = bf16[6,512,1024]{2,1,0:T(8,128)(2,1)} fusion(bf16[3,512,1024]{2,1,0:T(8,128)(2,1)} %get-tuple-element.29, bf16[3,512,1024]{2,1,0:T(8,128)(2,1)S(1)} %copy-done.4), kind=kLoop, calls=%fused_computation.4 | loop fusion | flops 3145728 | bytes 12582912 | tf_op jit(solution)/shard_map/concatenate | solution.py:28
  64.0 1.5 collective-permute-start.1
  65.5 1.3 collective-permute-start.8
  66.8 5.0 %fusion.12 = bf16[4,256,1024]{2,1,0:T(8,128)(2,1)} fusion(s32[]{:T(128)S(6)} %select_n.60, bf16[1,256,1024]{2,1,0:T(8,128)(2,1)S(1)} %bitcast.144, bf16[1,256,1024]{2,1,0:T(8,128)(2,1)} %bitcast.13, bf16[1,256,1024]{2,1,0:T(8,128)(2,1)} %bitcast.14, bf16[1,256,1024]{2,1,0:T(8,128)(2,1)} %bitcast.15), kind=kLoop, calls=%fused_computation.36 | loop fusion | flops 7340032 | bytes 4194308 | tf_op jit(solution)/shard_map/jit(_roll_dynamic)/concatenate | solution.py:42
  71.8 2.2 copy.72
  74.1 1.0 constant_dynamic-update-slice_fusion.2
  75.1 2.2 copy.73
  77.3 1.0 constant_dynamic-update-slice_fusion.1
  78.3 9.6 %collective-permute-done.8 = bf16[768,2,256]{2,1,0:T(2,128)(2,1)} collective-permute-done((bf16[768,2,256]{2,1,0:T(2,128)(2,1)}, bf16[768,2,256]{2,1,0:T(2,128)(2,1)}, u32[]{:S(2)}, u32[]{:S(2)}) %collective-permute-start.8) | collective-permute-done | bytes 786464 | tf_op jit(solution)/shard_map/ppermute | solution.py:20
  87.9 2.2 copy.74
  90.2 1.0 constant_dynamic-update-slice_fusion
  91.2 7.1 %convolution_convert_fusion.1 = bf16[1024,2,256]{0,2,1:T(8,128)(2,1)S(1)} fusion(bf16[3072,1024,1]{1,0,2:T(8,128)(2,1)} %bitcast.119, bf16[3072,2,256]{0,2,1:T(8,128)(2,1)} %constant_dynamic-update-slice_fusion), kind=kOutput, calls=%fused_computation.79 | convolution fusion | flops 3221749760 | bytes 10485760 | tf_op jit(solution)/shard_map/tf,fjc->tjc/dot_general | solution.py:101
  98.4 0.8 multiply_reduce_fusion.1
  99.3 2.0 copy-done.2
  101.3 1.6 fusion.38
  102.9 0.2 all-gather.5.cloned.1.call-start
  103.2 5.1 %fusion.19 = bf16[4,256,1024]{2,1,0:T(8,128)(2,1)} fusion(s32[]{:T(128)S(6)} %select_n.60, bf16[1,256,1024]{2,1,0:T(8,128)(2,1)S(1)} %bitcast.128, bf16[1,256,1024]{2,1,0:T(8,128)(2,1)} %bitcast.4, bf16[1,256,1024]{2,1,0:T(8,128)(2,1)} %bitcast.5, bf16[1,256,1024]{2,1,0:T(8,128)(2,1)} %bitcast.6), kind=kLoop, calls=%fused_computation.43 | loop fusion | flops 7340032 | bytes 4194308 | tf_op jit(solution)/shard_map/jit(_roll_dynamic)/concatenate | solution.py:42
  108.3 0.9 fusion.4
  109.2 13.2 %all-gather.1 = f32[8,2,512]{2,1,0:T(2,128)S(1)} all-gather(f32[2,2,512]{2,1,0:T(2,128)S(1)} %pad_maximum_fusion.1), channel_id=3, replica_groups=mesh['groups'=2,'picks'=4,'heads'=4] {'picks'}, dimensions={0}, use_global_device_ids=true | all-gather | bytes 40960 | tf_op jit(solution)/shard_map/all_gather | solution.py:115
  122.5 7.4 %all-gather.7.cloned.1.call-done = bf16[8,512,128]{2,1,0:T(8,128)(2,1)} async-done(((bf16[2,512,128]{2,1,0:T(8,128)(2,1)}), bf16[8,512,128]{2,1,0:T(8,128)(2,1)}) %all-gather.7.cloned.1.call-update) | async-done | bytes 1048592 | tf_op jit(solution)/shard_map/all_gather | solution.py:114
  129.9 1.8 multiply_reduce_fusion.2
  131.9 0.8 collective-permute-start.9
  132.8 0.7 collective-permute-start.10
  133.8 5.5 %collective-permute-done.9 = bf16[256,512]{1,0:T(8,128)(2,1)S(1)} collective-permute-done((bf16[256,512]{1,0:T(8,128)(2,1)S(1)}, bf16[256,512]{1,0:T(8,128)(2,1)S(1)}, u32[]{:S(2)}, u32[]{:S(2)}) %collective-permute-start.9) | collective-permute-done | bytes 262176 | tf_op jit(solution)/shard_map/ppermute | solution.py:40
  139.3 6.8 %collective-permute-done.10 = bf16[256,512]{1,0:T(8,128)(2,1)S(1)} collective-permute-done((bf16[256,512]{1,0:T(8,128)(2,1)S(1)}, bf16[256,512]{1,0:T(8,128)(2,1)S(1)}, u32[]{:S(2)}, u32[]{:S(2)}) %collective-permute-start.10) | collective-permute-done | bytes 262176 | tf_op jit(solution)/shard_map/ppermute | solution.py:40
  146.2 1.2 fusion.55
  147.4 2.6 %multiply_reduce_fusion.4 = (f32[512]{0:T(512)S(1)}, f32[512,1024]{1,0:T(8,128)S(1)}) fusion(bf16[1024,512]{1,0:T(8,128)(2,1)S(1)} %bitcast.124, bf16[1024,1024]{1,0:T(8,128)(2,1)S(1)} %bitcast.118, bf16[512,1024]{1,0:T(8,128)(2,1)} %param.19), kind=kOutput, calls=%fused_computation.73 | convolution fusion | flops 1075838464 | bytes 6293504 | tf_op jit(solution)/shard_map/dot_general | solution.py:133
  150.1 1.1 fusion.33
  151.3 0.5 fusion.29
  151.8 0.5 convolution_convert_fusion.5
  152.4 1.4 collective-permute-start.13
  154.1 4.1 %collective-permute-done.12 = bf16[256,512]{1,0:T(8,128)(2,1)S(1)} collective-permute-done((bf16[256,512]{1,0:T(8,128)(2,1)S(1)}, bf16[256,512]{1,0:T(8,128)(2,1)S(1)}, u32[]{:S(2)}, u32[]{:S(2)}) %collective-permute-start.12) | collective-permute-done | bytes 262176 | tf_op jit(solution)/shard_map/ppermute | solution.py:40
  158.2 8.2 %collective-permute-done.13 = bf16[256,512]{1,0:T(8,128)(2,1)S(1)} collective-permute-done((bf16[256,512]{1,0:T(8,128)(2,1)S(1)}, bf16[256,512]{1,0:T(8,128)(2,1)S(1)}, u32[]{:S(2)}, u32[]{:S(2)}) %collective-permute-start.13) | collective-permute-done | bytes 262176 | tf_op jit(solution)/shard_map/ppermute | solution.py:40
  166.6 1.2 fusion.48
  167.8 1.4 multiply_reduce_fusion.3
  169.2 1.3 copy-done.6
  170.6 0.8 fusion.37
  171.5 5.1 %convolution_convert_fusion.3 = bf16[1024,256]{0,1:T(8,128)(2,1)S(1)} fusion(bf16[3072,1024]{1,0:T(8,128)(2,1)} %bitcast.120, bf16[3072,256]{1,0:T(8,128)(2,1)} %all-gather.5.cloned.1.call-done), kind=kOutput, calls=%fused_computation.82 | convolution fusion | flops 1610874880 | bytes 8388608 | tf_op jit(solution)/shard_map/dot_general | solution.py:163
  176.6 0.8 fusion.3
  177.4 1.0 fusion.34
  178.5 0.2 fusion.77
  178.7 0.9 collective-permute-done.15
  179.6 0.8 collective-permute-start.16
  180.4 0.9 multiply_reduce_fusion
  181.3 2.0 collective-permute-done.16
  183.3 0.6 subtract_multiply_fusion
  183.9 1.2 multiply_convert_fusion.4
  185.1 0.3 slice-done.1
  185.4 3.1 %convolution_convert_fusion = bf16[3072,256]{1,0:T(8,128)(2,1)} fusion(bf16[3072,1024]{1,0:T(8,128)(2,1)S(1)} %bitcast.123, bf16[1024,256]{0,1:T(8,128)(2,1)S(1)} %bitcast.169), kind=kOutput, calls=%fused_computation.26 | convolution fusion | flops 1611399168 | bytes 8388608 | tf_op jit(solution)/shard_map/dot_general | solution.py:189
  188.6 1.9 constant_dynamic-slice_fusion
  190.5 32.4 %reduce-scatter.2.cloned.1.call-done = bf16[768,256]{1,0:T(8,128)(2,1)} async-done(((bf16[3072,256]{1,0:T(8,128)(2,1)}), bf16[768,256]{1,0:T(8,128)(2,1)}) %reduce-scatter.2.cloned.1.call-update) | async-done | bytes 393232 | tf_op jit(solution)/shard_map/reduce_scatter | solution.py:188
  222.9 1.9 convert_element_type.100
  (72 shorter events, 2.0 us)
Async XLA Ops:
  7.2 142.9 %copy-start = (bf16[3,1024,256]{2,1,0:T(8,128)(2,1)S(1)}, bf16[3,1024,256]{2,1,0:T(8,128)(2,1)}, u32[]{:S(2)}) copy-start(bf16[3,1024,256]{2,1,0:T(8,128)(2,1)} %param.23) | copy-start | bytes 4718596
  7.2 23.0 %copy-start.11 = (f32[3,1024]{1,0:T(4,128)S(1)}, f32[3,1024]{1,0:T(4,128)}, u32[]{:S(2)}) copy-start(f32[3,1024]{1,0:T(4,128)} %param.16) | copy-start | bytes 36868
  7.2 122.7 %all-gather.7.cloned.1.call-start = ((), (), s32[]{:S(2)}) async-start(), calls=%async_computation.3 | async-start | bytes 1310720 | tf_op jit(solution)/shard_map/all_gather | solution.py:114
  7.2 23.0 %collective-permute-start.6 = (bf16[768,2,256]{2,1,0:T(2,128)(2,1)}, bf16[768,2,256]{2,1,0:T(2,128)(2,1)}, u32[]{:S(2)}, u32[]{:S(2)}) collective-permute-start(bf16[768,2,256]{2,1,0:T(2,128)(2,1)} %param.20), channel_id=1, source_target_pairs={{0,4},{4,8},{8,12},{12,0},{1,5},{5,9},{9,13},{13,1},{2,6},{6,10},{... | collective-permute-start | bytes 2359304 | tf_op jit(solution)/shard_map/ppermute | solution.py:20
  10.3 53.6 %collective-permute-start.3 = (bf16[256,1024]{1,0:T(8,128)(2,1)}, bf16[256,1024]{1,0:T(8,128)(2,1)}, u32[]{:S(2)}, u32[]{:S(2)}) collective-permute-start(bf16[256,1024]{1,0:T(8,128)(2,1)} %param.21), channel_id=1, source_target_pairs={{0,3},{1,0},{2,1},{3,2},{4,7},{5,4},{6,5},{7,6},{8,11},{9,8},{10,9... | collective-permute-start | bytes 1572872 | tf_op jit(solution)/shard_map/ppermute | solution.py:40
  11.0 54.5 %collective-permute-start.4 = (bf16[256,1024]{1,0:T(8,128)(2,1)}, bf16[256,1024]{1,0:T(8,128)(2,1)}, u32[]{:S(2)}, u32[]{:S(2)}) collective-permute-start(bf16[256,1024]{1,0:T(8,128)(2,1)} %param.21), channel_id=1, source_target_pairs={{0,2},{1,3},{2,0},{3,1},{4,6},{5,7},{6,4},{7,5},{8,10},{9,11},{10,... | collective-permute-start | bytes 1572872 | tf_op jit(solution)/shard_map/ppermute | solution.py:40
  11.8 55.0 %collective-permute-start.5 = (bf16[256,1024]{1,0:T(8,128)(2,1)}, bf16[256,1024]{1,0:T(8,128)(2,1)}, u32[]{:S(2)}, u32[]{:S(2)}) collective-permute-start(bf16[256,1024]{1,0:T(8,128)(2,1)} %param.21), channel_id=1, source_target_pairs={{0,1},{1,2},{2,3},{3,0},{4,5},{5,6},{6,7},{7,4},{8,9},{9,10},{10,1... | collective-permute-start | bytes 1572872 | tf_op jit(solution)/shard_map/ppermute | solution.py:40
  13.3 89.9 %collective-permute-start = (bf16[256,1024]{1,0:T(8,128)(2,1)S(1)}, bf16[256,1024]{1,0:T(8,128)(2,1)}, u32[]{:S(2)}, u32[]{:S(2)}) collective-permute-start(bf16[256,1024]{1,0:T(8,128)(2,1)S(1)} %bitcast.125), channel_id=1, source_target_pairs={{0,3},{1,0},{2,1},{3,2},{4,7},{5,4},{6,5},{7,6},{8,11},{9,8},{10,9... | collective-permute-start | bytes 1572872 | tf_op jit(solution)/shard_map/ppermute | solution.py:40
  30.2 35.3 %collective-permute-start.7 = (bf16[768,2,256]{2,1,0:T(2,128)(2,1)}, bf16[768,2,256]{2,1,0:T(2,128)(2,1)}, u32[]{:S(2)}, u32[]{:S(2)}) collective-permute-start(bf16[768,2,256]{2,1,0:T(2,128)(2,1)} %collective-permute-done.6), channel_id=1, source_target_pairs={{0,4},{4,8},{8,12},{12,0},{1,5},{5,9},{9,13},{13,1},{2,6},{6,10},{... | collective-permute-start | bytes 2359304 | tf_op jit(solution)/shard_map/ppermute | solution.py:20
  55.8 3.0 %copy-start.4 = (bf16[3,512,1024]{2,1,0:T(8,128)(2,1)S(1)}, bf16[3,512,1024]{2,1,0:T(8,128)(2,1)}, u32[]{:S(2)}) copy-start(bf16[3,512,1024]{2,1,0:T(8,128)(2,1)} %get-tuple-element.28) | copy-start | bytes 9437188
  56.3 7.6 %copy-start.7 = (bf16[3072,2,256]{0,2,1:T(8,128)(2,1)}, bf16[3072,2,256]{0,2,1:T(8,128)(2,1)S(1)}, u32[]{:S(2)}) copy-start(bf16[3072,2,256]{0,2,1:T(8,128)(2,1)S(1)} %constant_dynamic-update-slice_fusion.3) | copy-start | bytes 9437188
  58.8 8.0 %copy-start.10 = (bf16[256,1024]{1,0:T(8,128)(2,1)S(1)}, bf16[256,1024]{1,0:T(8,128)(2,1)}, u32[]{:S(2)}) copy-start(bf16[256,1024]{1,0:T(8,128)(2,1)} %param.21) | copy-start | bytes 1572868
  64.0 39.2 %collective-permute-start.1 = (bf16[256,1024]{1,0:T(8,128)(2,1)S(1)}, bf16[256,1024]{1,0:T(8,128)(2,1)}, u32[]{:S(2)}, u32[]{:S(2)}) collective-permute-start(bf16[256,1024]{1,0:T(8,128)(2,1)S(1)} %bitcast.126), channel_id=1, source_target_pairs={{0,2},{1,3},{2,0},{3,1},{4,6},{5,7},{6,4},{7,5},{8,10},{9,11},{10,... | collective-permute-start | bytes 1572872 | tf_op jit(solution)/shard_map/ppermute | solution.py:40
  65.4 37.7 %collective-permute-start.2 = (bf16[256,1024]{1,0:T(8,128)(2,1)S(1)}, bf16[256,1024]{1,0:T(8,128)(2,1)}, u32[]{:S(2)}, u32[]{:S(2)}) collective-permute-start(bf16[256,1024]{1,0:T(8,128)(2,1)S(1)} %bitcast.127), channel_id=1, source_target_pairs={{0,1},{1,2},{2,3},{3,0},{4,5},{5,6},{6,7},{7,4},{8,9},{9,10},{10,1... | collective-permute-start | bytes 1572872 | tf_op jit(solution)/shard_map/ppermute | solution.py:40
  65.5 22.5 %collective-permute-start.8 = (bf16[768,2,256]{2,1,0:T(2,128)(2,1)}, bf16[768,2,256]{2,1,0:T(2,128)(2,1)}, u32[]{:S(2)}, u32[]{:S(2)}) collective-permute-start(bf16[768,2,256]{2,1,0:T(2,128)(2,1)} %collective-permute-done.7), channel_id=1, source_target_pairs={{0,4},{4,8},{8,12},{12,0},{1,5},{5,9},{9,13},{13,1},{2,6},{6,10},{... | collective-permute-start | bytes 2359304 | tf_op jit(solution)/shard_map/ppermute | solution.py:20
  99.3 2.1 copy-start.2
  102.9 68.6 %all-gather.5.cloned.1.call-start = ((), (), s32[]{:S(2)}) async-start(), calls=%async_computation.1 | async-start | bytes 1966080 | tf_op jit(solution)/shard_map/all_gather | solution.py:131
  103.2 5.1 %copy-start.3 = (f32[2,512,1024]{2,1,0:T(8,128)S(1)}, f32[2,512,1024]{2,1,0:T(8,128)}, u32[]{:S(2)}) copy-start(f32[2,512,1024]{2,1,0:T(8,128)} %copy-done.2) | copy-start | bytes 12582916
  109.2 24.5 %copy-start.12 = (f32[2,1024]{1,0:T(2,128)S(1)}, f32[2,1024]{1,0:T(2,128)}, u32[]{:S(2)}) copy-start(f32[2,1024]{1,0:T(2,128)} %param.22) | copy-start | bytes 24580
  131.9 7.3 %collective-permute-start.9 = (bf16[256,512]{1,0:T(8,128)(2,1)S(1)}, bf16[256,512]{1,0:T(8,128)(2,1)S(1)}, u32[]{:S(2)}, u32[]{:S(2)}) collective-permute-start(bf16[256,512]{1,0:T(8,128)(2,1)S(1)} %bitcast.131), channel_id=1, source_target_pairs={{0,3},{1,0},{2,1},{3,2},{4,7},{5,4},{6,5},{7,6},{8,11},{9,8},{10,9... | collective-permute-start | bytes 786440 | tf_op jit(solution)/shard_map/ppermute | solution.py:40
  132.8 13.3 %collective-permute-start.10 = (bf16[256,512]{1,0:T(8,128)(2,1)S(1)}, bf16[256,512]{1,0:T(8,128)(2,1)S(1)}, u32[]{:S(2)}, u32[]{:S(2)}) collective-permute-start(bf16[256,512]{1,0:T(8,128)(2,1)S(1)} %bitcast.132), channel_id=1, source_target_pairs={{0,2},{1,3},{2,0},{3,1},{4,6},{5,7},{6,4},{7,5},{8,10},{9,11},{10,... | collective-permute-start | bytes 786440 | tf_op jit(solution)/shard_map/ppermute | solution.py:40
  133.5 12.7 %collective-permute-start.11 = (bf16[256,512]{1,0:T(8,128)(2,1)S(1)}, bf16[256,512]{1,0:T(8,128)(2,1)S(1)}, u32[]{:S(2)}, u32[]{:S(2)}) collective-permute-start(bf16[256,512]{1,0:T(8,128)(2,1)S(1)} %bitcast.133), channel_id=1, source_target_pairs={{0,1},{1,2},{2,3},{3,0},{4,5},{5,6},{6,7},{7,4},{8,9},{9,10},{10,1... | collective-permute-start | bytes 786440 | tf_op jit(solution)/shard_map/ppermute | solution.py:40
  133.7 89.2 %reduce-scatter.2.cloned.1.call-start = ((), (), s32[]{:S(2)}) async-start(), calls=%async_computation.2 | async-start | bytes 1966080 | tf_op jit(solution)/shard_map/reduce_scatter | solution.py:188
  133.7 13.7 %copy-start.5 = (bf16[4,256,1024]{2,1,0:T(8,128)(2,1)S(1)}, bf16[4,256,1024]{2,1,0:T(8,128)(2,1)}, u32[]{:S(2)}) copy-start(bf16[4,256,1024]{2,1,0:T(8,128)(2,1)} %fusion.12) | copy-start | bytes 6291460
  151.8 2.2 copy-start.13
  151.8 2.2 copy-start.15
  152.3 15.5 %copy-start.8 = (bf16[4,256,1024]{2,1,0:T(8,128)(2,1)S(1)}, bf16[4,256,1024]{2,1,0:T(8,128)(2,1)}, u32[]{:S(2)}) copy-start(bf16[4,256,1024]{2,1,0:T(8,128)(2,1)} %fusion.19) | copy-start | bytes 6291460
  152.4 5.8 %collective-permute-start.12 = (bf16[256,512]{1,0:T(8,128)(2,1)S(1)}, bf16[256,512]{1,0:T(8,128)(2,1)S(1)}, u32[]{:S(2)}, u32[]{:S(2)}) collective-permute-start(bf16[256,512]{1,0:T(8,128)(2,1)S(1)} %bitcast.149), channel_id=1, source_target_pairs={{0,3},{1,0},{2,1},{3,2},{4,7},{5,4},{6,5},{7,6},{8,11},{9,8},{10,9... | collective-permute-start | bytes 786440 | tf_op jit(solution)/shard_map/ppermute | solution.py:40
  152.4 13.9 %collective-permute-start.13 = (bf16[256,512]{1,0:T(8,128)(2,1)S(1)}, bf16[256,512]{1,0:T(8,128)(2,1)S(1)}, u32[]{:S(2)}, u32[]{:S(2)}) collective-permute-start(bf16[256,512]{1,0:T(8,128)(2,1)S(1)} %bitcast.150), channel_id=1, source_target_pairs={{0,2},{1,3},{2,0},{3,1},{4,6},{5,7},{6,4},{7,5},{8,10},{9,11},{10,... | collective-permute-start | bytes 786440 | tf_op jit(solution)/shard_map/ppermute | solution.py:40
  153.9 12.7 %collective-permute-start.14 = (bf16[256,512]{1,0:T(8,128)(2,1)S(1)}, bf16[256,512]{1,0:T(8,128)(2,1)S(1)}, u32[]{:S(2)}, u32[]{:S(2)}) collective-permute-start(bf16[256,512]{1,0:T(8,128)(2,1)S(1)} %bitcast.151), channel_id=1, source_target_pairs={{0,1},{1,2},{2,3},{3,0},{4,5},{5,6},{6,7},{7,4},{8,9},{9,10},{10,1... | collective-permute-start | bytes 786440 | tf_op jit(solution)/shard_map/ppermute | solution.py:40
  167.8 2.8 %copy-start.9 = (bf16[2,1024,256]{2,1,0:T(8,128)(2,1)S(1)}, bf16[2,1024,256]{2,1,0:T(8,128)(2,1)}, u32[]{:S(2)}) copy-start(bf16[2,1024,256]{2,1,0:T(8,128)(2,1)} %param.25) | copy-start | bytes 3145732
  169.2 1.4 copy-start.6
  176.6 0.9 copy-start.14
  178.4 1.2 collective-permute-start.15
  179.6 3.6 %collective-permute-start.16 = (f32[1024]{0:T(1024)S(1)}, f32[1024]{0:T(1024)S(1)}, u32[]{:S(2)}, u32[]{:S(2)}) collective-permute-start(f32[1024]{0:T(1024)S(1)} %add.93), channel_id=1, source_target_pairs={{0,2},{1,3},{2,0},{3,1},{4,6},{5,7},{6,4},{7,5},{8,10},{9,11},{10,... | collective-permute-start | bytes 12296 | tf_op jit(solution)/shard_map/ppermute | solution.py:68
  180.4 4.7 %slice-start = ((s8[6291456]{0:T(1024)(128)(4,1)}), s8[4194304]{0:T(1024)(128)(4,1)S(1)}, s32[]{:S(2)}) async-start(s8[6291456]{0:T(1024)(128)(4,1)} %bitcast.121), calls=%async_computation.4 | async-start | bytes 8388608
  183.9 1.6 slice-start.1
  185.4 39.4 %copy-start.1 = (bf16[3,1024,256]{2,1,0:T(8,128)(2,1)S(1)}, bf16[3,1024,256]{2,1,0:T(8,128)(2,1)}, u32[]{:S(2)}) copy-start(bf16[3,1024,256]{2,1,0:T(8,128)(2,1)} %param.23) | copy-start | bytes 4718596
Sparse Core Ops, SparseCore 0:
  103.0 26.8 all-gather.6
  133.8 36.9 all-gather.4
  188.7 34.1 reduce-scatter.1
